TPU v7x, 32 devices: a whole 2x2x4 slice. The times are simulated.
32 devices in a mesh: groups: 2 (over y), seq: 8 (over z, x), wg: 2 (over core).
Axes of the slice: x: 2, y: 2, z: 4, core: 2. Of those that a mesh axis runs over, the one named last changes fastest.
Arguments:
- generator_rows: bfloat16 [2048, 2304], P(('groups', 'seq'), 'wg'), parts along dimension 0, may hold values from -120 to 120, as said below
- pre_gain: float32 [2304], replicated, may hold values from 0.1 to 1.9
- query_weight: bfloat16 [2304, 2048], P('seq', 'wg'), may hold values from -2 to 2, as said below
- key_weight: bfloat16 [2304, 1024], P('seq', 'wg'), may hold values from -2 to 2, as said below
- value_weight: bfloat16 [2304, 1024], P('seq', 'wg'), may hold values from -0.125 to 0.125
- out_weight: bfloat16 [2048, 2304], P('wg', 'seq'), may hold values from -0.125 to 0.125
- post_gain: float32 [2304], replicated, may hold values from 0.1 to 1.9
- final_gain: float32 [2304], replicated, may hold values from 0.1 to 1.9
- label_table: bfloat16 [64, 2304], replicated, may hold values from -0.375 to 0.375
- lengths: int32 [16], P('groups'), parts along dimension 0, may hold values from 65 to 127
- label_index: int32 [16], P('groups'), parts along dimension 0, may hold values from 0 to 63
Outputs:
- input_grad: bfloat16 [2048, 2304], P(('groups', 'seq'), 'wg'), parts along dimension 0
There are 2 independent parts, one for each index of `groups`. A program takes and returns all parts, laid end to end along the dimension named above; an argument that names none is the same for every part. Nothing has to cross between parts.
Inputs may be any that keep to these rules, and one draw needn't show every extreme that they name: `generator_rows`: finite real entries. `query_weight`: finite real entries. `key_weight`: finite real entries.
All inputs are finite; a program needn't handle non-finite values.
Results may differ from a plain program's by a relative error of at most 0.017.
The roundings to bfloat16 on the way count: a program that leaves them out, or rounds other values in their place, can miss the bound.
Values may be sent and summed in bfloat16 or wider, within the bound.
No kernel may reach another device: no remote copies, remote signals or barrier semaphores. Data moves between devices by JAX's collectives and lax.ppermute only.
A program may use at most 128 MiB of HBM per device.

v0:
```python
import jax
import jax.numpy as jnp
from jax import lax
from jax.sharding import PartitionSpec as P

HD = 128
LABELS = 64
EPSILON = 1e-06
ATTEND_CAP = 50.0
LABEL_CAP = 30.0
QUERY_SCALE = 1.0 / 12.0


def rope_tables(positions, head_width):
    frequency = 10000.0 ** (-2.0 * jnp.arange(head_width // 2, dtype=jnp.float32) / head_width)
    angles = positions.astype(jnp.float32)[:, None] * frequency[None, :]
    return (jnp.cos(angles), jnp.sin(angles))


def rotate(values, cos_table, sin_table):
    half_width = values.shape[-1] // 2
    lower_part = values[..., :half_width]
    upper_part = values[..., half_width:]
    return jnp.concatenate(
        [
            lower_part * cos_table - upper_part * sin_table,
            upper_part * cos_table + lower_part * sin_table,
        ],
        axis=-1,
    )


def rotate_back(values, cos_table, sin_table):
    half_width = values.shape[-1] // 2
    lower_part = values[..., :half_width]
    upper_part = values[..., half_width:]
    return jnp.concatenate(
        [
            lower_part * cos_table + upper_part * sin_table,
            upper_part * cos_table - lower_part * sin_table,
        ],
        axis=-1,
    )


def times_transposed(left_side, right_side):
    return lax.dot_general(
        left_side, right_side, (((1,), (1,)), ((), ())), preferred_element_type=jnp.float32
    )


def shards(
    generator_rows,
    pre_gain,
    query_weight,
    key_weight,
    value_weight,
    out_weight,
    post_gain,
    final_gain,
    label_table,
    lengths,
    label_index,
):
    seq_rank = lax.axis_index("seq")
    core_rank = lax.axis_index("wg")
    whole_rows = lax.all_gather(generator_rows, "wg", axis=1, tiled=True)
    guard_rows = lax.all_to_all(whole_rows, "seq", split_axis=0, concat_axis=0, tiled=True)
    w_query, w_key, w_value, w_out = (
        lax.all_gather(query_weight, "seq", axis=0, tiled=True),
        lax.all_gather(key_weight, "seq", axis=0, tiled=True),
        lax.all_gather(value_weight, "seq", axis=0, tiled=True),
        lax.all_gather(out_weight, "seq", axis=1, tiled=True),
    )
    tok_rows = guard_rows.shape[0]
    half_width = generator_rows.shape[1]
    local_heads = w_query.shape[1] // HD
    local_kv = w_key.shape[1] // HD
    group_size = local_heads // local_kv
    length = lax.dynamic_index_in_dim(lengths, seq_rank, 0, keepdims=False)
    target = lax.dynamic_index_in_dim(label_index, seq_rank, 0, keepdims=False)
    offsets = jnp.arange(tok_rows, dtype=jnp.int32)
    cos_table, sin_table = rope_tables(offsets, HD)
    inputs = guard_rows.astype(jnp.float32)
    scale_in = lax.rsqrt(jnp.mean(inputs * inputs, axis=-1, keepdims=True) + EPSILON)
    normed = (inputs * scale_in * pre_gain).astype(jnp.bfloat16)
    query_proj = (
        jnp.dot(normed, w_query, preferred_element_type=jnp.float32)
        .reshape(tok_rows, local_heads, HD)
        .transpose(1, 0, 2)
    )
    queries = (rotate(query_proj, cos_table, sin_table) * QUERY_SCALE).astype(jnp.bfloat16)
    key_proj = (
        jnp.dot(normed, w_key, preferred_element_type=jnp.float32)
        .reshape(tok_rows, local_kv, HD)
        .transpose(1, 0, 2)
    )
    keys_own = rotate(key_proj, cos_table, sin_table).astype(jnp.bfloat16)
    values_own = (
        jnp.dot(normed, w_value, preferred_element_type=jnp.float32)
        .astype(jnp.bfloat16)
        .reshape(tok_rows, local_kv, HD)
        .transpose(1, 0, 2)
    )
    allowed = (offsets[None, :] <= offsets[:, None]) & (offsets[None, :] < length)
    query_four = queries.reshape(local_kv, group_size, tok_rows, HD)
    raw_scores = jnp.einsum(
        "kgid,kjd->kgij", query_four, keys_own, preferred_element_type=jnp.float32
    )
    capped = jnp.tanh(raw_scores / ATTEND_CAP)
    weight_exp = jnp.where(allowed[None, None], jnp.exp(ATTEND_CAP * capped), 0.0)
    soft_weights = weight_exp / jnp.sum(weight_exp, axis=-1, keepdims=True)
    attend = soft_weights.astype(jnp.bfloat16)
    context = jnp.einsum(
        "kgij,kjd->kgid", attend, values_own, preferred_element_type=jnp.float32
    ).astype(jnp.bfloat16)
    context_rows = (
        context.reshape(local_heads, tok_rows, HD)
        .transpose(1, 0, 2)
        .reshape(tok_rows, local_heads * HD)
    )
    out_part = jnp.dot(context_rows, w_out, preferred_element_type=jnp.float32)
    attention = lax.psum(out_part.astype(jnp.bfloat16), "wg").astype(jnp.float32)
    scale_attn = lax.rsqrt(jnp.mean(attention * attention, axis=-1, keepdims=True) + EPSILON)
    mixed_rows = inputs + attention * scale_attn * post_gain
    scale_out = lax.rsqrt(jnp.mean(mixed_rows * mixed_rows, axis=-1, keepdims=True) + EPSILON)
    final_rows = (mixed_rows * scale_out * final_gain).astype(jnp.bfloat16)
    logits = times_transposed(final_rows, label_table)
    label_cap = jnp.tanh(logits / LABEL_CAP)
    label_exp = jnp.exp(LABEL_CAP * label_cap)
    chance = label_exp / jnp.sum(label_exp, axis=-1, keepdims=True)
    live_rows = (offsets < length)[:, None]
    onehot = (jnp.arange(LABELS, dtype=jnp.int32) == target).astype(jnp.float32)[None, :]
    grad_logit = (
        jnp.where(live_rows, chance - onehot, 0.0) * (1.0 - label_cap * label_cap)
    ).astype(jnp.bfloat16)
    grad_final = jnp.dot(grad_logit, label_table, preferred_element_type=jnp.float32)
    scaled_final = grad_final * final_gain
    cube_out = scale_out * scale_out * scale_out
    grad_mixed = scale_out * scaled_final - mixed_rows * cube_out * jnp.mean(
        scaled_final * mixed_rows, axis=-1, keepdims=True
    )
    scaled_post = grad_mixed * post_gain
    cube_attn = scale_attn * scale_attn * scale_attn
    grad_attention = scale_attn * scaled_post - attention * cube_attn * jnp.mean(
        scaled_post * attention, axis=-1, keepdims=True
    )
    grad_context = times_transposed(grad_attention.astype(jnp.bfloat16), w_out).astype(jnp.bfloat16)
    grad_four = grad_context.reshape(tok_rows, local_kv, group_size, HD).transpose(1, 2, 0, 3)
    grad_prob = jnp.einsum(
        "kgid,kjd->kgij", grad_four, values_own, preferred_element_type=jnp.float32
    )
    grad_score = (
        soft_weights
        * (grad_prob - jnp.sum(soft_weights * grad_prob, axis=-1, keepdims=True))
        * (1.0 - capped * capped)
    )
    score_round = grad_score.astype(jnp.bfloat16)
    grad_query = jnp.einsum(
        "kgij,kjd->kgid", score_round, keys_own, preferred_element_type=jnp.float32
    ).reshape(local_heads, tok_rows, HD)
    grad_queries = rotate_back(grad_query * QUERY_SCALE, cos_table, sin_table).astype(jnp.bfloat16)
    grad_key = jnp.einsum(
        "kgij,kgid->kjd", score_round, query_four, preferred_element_type=jnp.float32
    )
    grad_value = jnp.einsum("kgij,kgid->kjd", attend, grad_four, preferred_element_type=jnp.float32)
    grad_keys = rotate_back(grad_key, cos_table, sin_table).astype(jnp.bfloat16)
    grad_values = grad_value.astype(jnp.bfloat16)
    query_rows = grad_queries.transpose(1, 0, 2).reshape(tok_rows, local_heads * HD)
    key_rows = grad_keys.transpose(1, 0, 2).reshape(tok_rows, local_kv * HD)
    value_rows = grad_values.transpose(1, 0, 2).reshape(tok_rows, local_kv * HD)
    grad_part = (
        times_transposed(query_rows, w_query)
        + times_transposed(key_rows, w_key)
        + times_transposed(value_rows, w_value)
    )
    cube_in = scale_in * scale_in * scale_in
    grad_normed = lax.psum(grad_part.astype(jnp.bfloat16), "wg").astype(jnp.float32)
    scaled_in = grad_normed * pre_gain
    row_stat = jnp.mean(scaled_in * inputs, axis=-1, keepdims=True)
    grad_full = scale_in * scaled_in - inputs * cube_in * row_stat + grad_mixed
    grad_rows = lax.dynamic_slice_in_dim(grad_full, core_rank * half_width, half_width, 1)
    return lax.all_to_all(
        grad_rows.astype(jnp.bfloat16), "seq", split_axis=0, concat_axis=0, tiled=True
    )


def solution(mesh):
    return jax.shard_map(
        shards,
        mesh=mesh,
        in_specs=(
            P(("groups", "seq"), "wg"),
            P(),
            P("seq", "wg"),
            P("seq", "wg"),
            P("seq", "wg"),
            P("wg", "seq"),
            P(),
            P(),
            P(),
            P("groups"),
            P("groups"),
        ),
        out_specs=P(("groups", "seq"), "wg"),
        check_vma=False,
    )
```

profile of v0, /device:TPU:0, one launch (start us, length us, event | category | flops | bytes accessed | tf_op | source)
XLA Modules:
  0.0 376.7 jit_solution(12886535654456239035)
XLA Ops:
  6.5 0.7 all-gather.7.cloned.1.call-update
  7.3 0.7 all-gather.9.cloned.1.call-update
  8.1 0.7 all-gather.5.cloned.1.call-update
  8.8 0.5 all-gather.11.cloned.1.call-update
  9.4 2.4 all_gather.15
  11.8 7.2 %all-to-all-start = ((bf16[8,16,2304]{2,1,0:T(8,128)(2,1)}), bf16[8,16,2304]{2,1,0:T(8,128)(2,1)S(1)}, u32[]{:S(2)}, u32[]{:S(2)}) async-start(bf16[8,16,2304]{2,1,0:T(8,128)(2,1)} %bitcast), calls=%async_computation | async-start | bytes 1179648 | tf_op jit(solution)/shard_map/all_to_all | solution.py:68
  19.0 0.6 dynamic_slice.10
  19.6 0.7 iota_compare_fusion.1
  20.6 24.1 %all-to-all-done = bf16[8,16,2304]{2,1,0:T(8,128)(2,1)S(1)} async-done(((bf16[8,16,2304]{2,1,0:T(8,128)(2,1)}), bf16[8,16,2304]{2,1,0:T(8,128)(2,1)S(1)}, u32[]{:S(2)}, u32[]{:S(2)}) %all-to-all-start) | async-done | bytes 589856 | tf_op jit(solution)/shard_map/all_to_all | solution.py:68
  44.9 1.0 multiply_convert_fusion.2
  46.0 1.2 bitcast_convert_fusion
  47.1 25.5 %all-gather.7.cloned.1.call-done = bf16[2304,512]{1,0:T(8,128)(2,1)} async-done(((bf16[288,512]{1,0:T(8,128)(2,1)}), bf16[2304,512]{1,0:T(8,128)(2,1)}) %all-gather.7.cloned.1.call-update) | async-done | bytes 2359312 | tf_op jit(solution)/shard_map/all_gather | solution.py:71
  72.7 2.8 copy.15
  75.5 50.0 %all-gather.9.cloned.1.call-done = bf16[2304,512]{1,0:T(8,128)(2,1)} async-done(((bf16[288,512]{1,0:T(8,128)(2,1)}), bf16[2304,512]{1,0:T(8,128)(2,1)}) %all-gather.9.cloned.1.call-update) | async-done | bytes 2359312 | tf_op jit(solution)/shard_map/all_gather | solution.py:72
  125.5 2.5 convolution_convert_fusion.3
  128.1 0.7 copy.50
  128.8 1.8 convolution_bitcast_fusion.3
  130.7 75.5 %all-gather.5.cloned.1.call-done = bf16[2304,1024]{1,0:T(8,128)(2,1)} async-done(((bf16[288,1024]{1,0:T(8,128)(2,1)}), bf16[2304,1024]{1,0:T(8,128)(2,1)}) %all-gather.5.cloned.1.call-update) | async-done | bytes 4718608 | tf_op jit(solution)/shard_map/all_gather | solution.py:70
  206.1 6.8 %copy.12 = bf16[1024,2304]{1,0:T(8,128)(2,1)} copy(bf16[1024,2304]{0,1:T(8,128)(2,1)} %bitcast.103) | data formatting | bytes 9437184 | tf_op jit(solution)/shard_map/dot_general | solution.py:88
  213.0 4.0 %convolution_bitcast_fusion = f32[8,128,128]{1,2,0:T(8,128)S(1)} fusion(bf16[128,2304,1]{1,0,2:T(8,128)(2,1)S(1)} %bitcast.108, bf16[8,128,2304]{2,1,0:T(8,128)(2,1)} %bitcast.104), kind=kOutput, calls=%fused_computation.16 | convolution fusion | flops 603979776 | bytes 5832704 | tf_op jit(solution)/shard_map/dot_general | solution.py:88
  217.7 0.4 fusion.34
  218.1 0.3 copy-done.11
  218.4 0.3 convolution_convert_fusion.1
  218.7 0.2 copy-done.19
  218.9 67.3 %all-gather.11.cloned.1.call-done = bf16[1024,2304]{0,1:T(8,128)(2,1)} async-done(((bf16[1024,288]{0,1:T(8,128)(2,1)}), bf16[1024,2304]{0,1:T(8,128)(2,1)}) %all-gather.11.cloned.1.call-update) | async-done | bytes 4718608 | tf_op jit(solution)/shard_map/all_gather | solution.py:73
  286.3 4.9 %convolution_convert_fusion = bf16[128,2304]{1,0:T(8,128)(2,1)} fusion(bf16[128,1024]{0,1:T(8,128)(2,1)S(1)} %bitcast.118, bf16[1024,2304]{0,1:T(8,128)(2,1)} %all-gather.11.cloned.1.call-done), kind=kOutput, calls=%fused_computation.5 | convolution fusion | flops 604274688 | bytes 5570560 | tf_op jit(solution)/shard_map/dot_general | solution.py:122
  291.4 0.6 dynamic_slice.11
  292.0 0.6 compare_convert_fusion
  292.7 15.7 %all-reduce.3.cloned.1.call-done = bf16[128,2304]{1,0:T(8,128)(2,1)} async-done(((bf16[128,2304]{1,0:T(8,128)(2,1)}), bf16[128,2304]{1,0:T(8,128)(2,1)}) %all-reduce.3.cloned.1.call-update) | async-done | bytes 589840 | tf_op jit(solution)/shard_map/psum | solution.py:123
  308.3 1.3 fusion.7
  309.6 1.5 multiply_reduce_fusion.2
  311.1 0.4 fusion.43
  311.6 0.5 multiply_reduce_fusion.1
  312.2 0.5 fusion.13
  312.7 1.3 copy-done.1
  314.0 1.2 convolution_convert_fusion.2
  315.4 2.0 fusion.14
  317.7 1.7 convolution_bitcast_fusion.2
  319.4 2.6 convolution_multiply_fusion.1
  322.0 1.2 copy.24
  323.4 4.2 %fusion.66 = f32[128,2304]{1,0:T(8,128)S(1)} fusion(bf16[128,1024]{0,1:T(8,128)(2,1)S(1)} %bitcast.116, bf16[2304,1024]{1,0:T(8,128)(2,1)} %all-gather.5.cloned.1.call-done), kind=kOutput, calls=%fused_computation.121 | convolution fusion | flops 603979776 | bytes 6160384 | tf_op jit(solution)/shard_map/dot_general | solution.py:47
  327.6 0.9 convolution_add_fusion.1
  328.6 0.7 copy-done.4
  329.3 1.7 fusion.1
  331.1 20.2 %all-reduce.5.cloned.1.call-done = bf16[128,2304]{1,0:T(8,128)(2,1)} async-done(((bf16[128,2304]{1,0:T(8,128)(2,1)}), bf16[128,2304]{1,0:T(8,128)(2,1)}) %all-reduce.5.cloned.1.call-update) | async-done | bytes 589840 | tf_op jit(solution)/shard_map/psum | solution.py:178
  351.2 1.3 multiply_reduce_fusion
  352.8 16.4 %all_to_all.21 = bf16[8,16,1152]{2,1,0:T(8,128)(2,1)S(1)} all-to-all(bf16[8,16,1152]{2,1,0:T(8,128)(2,1)S(1)} %bitcast.110), channel_id=1, replica_groups=mesh['groups'=2,'seq'=8,'wg'=2] {'seq'}, dimensions={0} | all-to-all | bytes 589824 | tf_op jit(solution)/shard_map/all_to_all | solution.py:183
  369.2 0.7 copy.54
  (73 shorter events, 2.7 us)
Async XLA Ops:
  6.5 304.6 %copy-start = (bf16[64,2304]{1,0:T(8,128)(2,1)S(1)}, bf16[64,2304]{1,0:T(8,128)(2,1)}, u32[]{:S(2)}) copy-start(bf16[64,2304]{1,0:T(8,128)(2,1)} %param.19) | copy-start | bytes 884740
  6.5 2.8 copy-start.7
  6.5 66.1 %all-gather.7.cloned.1.call-start = ((), (), s32[]{:S(2)}) async-start(), calls=%async_computation.3 | async-start | bytes 2654208 | tf_op jit(solution)/shard_map/all_gather | solution.py:71
  7.3 118.2 %all-gather.9.cloned.1.call-start = ((), (), s32[]{:S(2)}) async-start(), calls=%async_computation.4 | async-start | bytes 2654208 | tf_op jit(solution)/shard_map/all_gather | solution.py:72
  8.0 198.1 %all-gather.5.cloned.1.call-start = ((), (), s32[]{:S(2)}) async-start(), calls=%async_computation.2 | async-start | bytes 5308416 | tf_op jit(solution)/shard_map/all_gather | solution.py:70
  8.7 277.5 %all-gather.11.cloned.1.call-start = ((), (), s32[]{:S(2)}) async-start(), calls=%async_computation.5 | async-start | bytes 5308416 | tf_op jit(solution)/shard_map/all_gather | solution.py:73
  9.3 9.7 %copy-start.17 = (s32[8]{0:T(128)S(1)}, s32[8]{0:T(128)}, u32[]{:S(2)}) copy-start(s32[8]{0:T(128)} %param.20) | copy-start | bytes 100
  9.3 35.6 %copy-start.12 = (f32[2304]{0:T(1024)S(1)}, f32[2304]{0:T(1024)}, u32[]{:S(2)}) copy-start(f32[2304]{0:T(1024)} %param.12) | copy-start | bytes 27652
  11.8 32.8 %all-to-all-start = ((bf16[8,16,2304]{2,1,0:T(8,128)(2,1)}), bf16[8,16,2304]{2,1,0:T(8,128)(2,1)S(1)}, u32[]{:S(2)}, u32[]{:S(2)}) async-start(bf16[8,16,2304]{2,1,0:T(8,128)(2,1)} %bitcast), calls=%async_computation | async-start | bytes 1179648 | tf_op jit(solution)/shard_map/all_to_all | solution.py:68
  19.0 289.3 %all-reduce.3.cloned.1.call-start = ((), (), s32[]{:S(2)}) async-start(), calls=%async_computation.6 | async-start | bytes 1179648 | tf_op jit(solution)/shard_map/psum | solution.py:123
  130.7 87.0 %copy-start.14 = (bf16[4,128,64]{1,2,0:T(8,128)(2,1)}, bf16[4,128,64]{1,2,0:T(8,128)(2,1)S(1)}, u32[]{:S(2)}) copy-start(bf16[4,128,64]{1,2,0:T(8,128)(2,1)S(1)} %get-tuple-element.18) | copy-start | bytes 196612
  206.1 6.8 %copy-start.6 = (bf16[8,16,2304]{2,1,0:T(8,128)(2,1)S(1)}, bf16[8,16,2304]{2,1,0:T(8,128)(2,1)}, u32[]{:S(2)}) copy-start(bf16[8,16,2304]{2,1,0:T(8,128)(2,1)} %multiply_convert_fusion.2) | copy-start | bytes 1769476
  217.5 0.9 copy-start.11
  217.7 1.0 copy-start.8
  218.1 0.8 copy-start.19
  218.1 0.8 copy-start.20
  286.3 5.2 %copy-start.18 = (s32[8]{0:T(128)S(1)}, s32[8]{0:T(128)}, u32[]{:S(2)}) copy-start(s32[8]{0:T(128)} %param.21) | copy-start | bytes 100
  291.1 18.4 %copy-start.13 = (f32[2304]{0:T(1024)S(1)}, f32[2304]{0:T(1024)}, u32[]{:S(2)}) copy-start(f32[2304]{0:T(1024)} %param.17) | copy-start | bytes 27652
  291.2 60.1 %all-reduce.5.cloned.1.call-start = ((), (), s32[]{:S(2)}) async-start(), calls=%async_computation.7 | async-start | bytes 1179648 | tf_op jit(solution)/shard_map/psum | solution.py:178
  309.6 1.5 copy-start.16
  311.1 1.1 copy-start.2
  311.6 2.4 copy-start.1
  314.0 1.4 copy-start.21
  315.4 2.2 copy-start.9
  317.7 1.8 copy-start.15
  323.4 4.2 %copy-start.3 = (bf16[2304,512]{1,0:T(8,128)(2,1)S(1)}, bf16[2304,512]{1,0:T(8,128)(2,1)}, u32[]{:S(2)}) copy-start(bf16[2304,512]{1,0:T(8,128)(2,1)} %all-gather.7.cloned.1.call-done) | copy-start | bytes 7077892
  327.6 1.7 copy-start.4
  327.6 1.7 copy-start.10
  331.1 21.5 %copy-start.5 = (f32[128,2304]{1,0:T(8,128)S(1)}, f32[128,2304]{1,0:T(8,128)}, u32[]{:S(2)}) copy-start(f32[128,2304]{1,0:T(8,128)} %bitcast_convert_fusion) | copy-start | bytes 3538948
Sparse Core Ops, SparseCore 0:
  9.5 63.0 all-gather.6
  74.9 50.6 all-gather.8
  127.7 78.4 all-gather.4
  208.2 78.0 all-gather.10
  291.3 16.9 all-reduce.2
  331.2 20.0 all-reduce.4
where the time goes:
time: 378 us; the launch traced here: 377 us
  waiting for transfers between devices  281 us (74%)
  matrix products  29.5 us (8%)
  blocking collectives  18.8 us (5%)
  local copies, waits for them, and re-layouts  16.9 us (4%)
  between operations  13.9 us (4%)
  other arithmetic  9.24 us (2%)
  starting transfers between devices  7.55 us (2%)
    all_gather x1, waiting for transfers between devices, shards(): lax.all_gather(query_weight, 'seq', axis=0, tiled=True)  75.5 us
    all_gather x1, waiting for transfers between devices, shards(): lax.all_gather(out_weight, 'seq', axis=1, tiled=True)  67.3 us
    all_gather x1, waiting for transfers between devices, shards(): lax.all_gather(value_weight, 'seq', axis=0, tiled=True)  50 us
    all_gather x1, waiting for transfers between devices, shards(): lax.all_gather(key_weight, 'seq', axis=0, tiled=True)  25.5 us
    all_to_all x1, waiting for transfers between devices, shards(): lax.all_to_all(whole_rows, 'seq', split_axis=0, concat_axis=0, tiled=True)  24.1 us
    psum x1, waiting for transfers between devices, shards(): lax.psum(grad_part.astype(jnp.bfloat16), 'wg').astype(jnp.float32)  20.2 us
    all_to_all x1, blocking collectives, shards(): lax.all_to_all(grad_rows.astype(jnp.bfloat16), 'seq', split_axis=0, conca...  16.4 us
    psum x1, waiting for transfers between devices, shards(): lax.psum(out_part.astype(jnp.bfloat16), 'wg').astype(jnp.float32)  15.7 us
  transfers between devices with their start and end apart: 7, of which 7 were waited for; matrix products, arithmetic and copies ran while one was open for 7% of the time, Pallas kernels for 0%

commit v1 on v0

--- a/solution.py
+++ b/solution.py
@@ -9,6 +9,18 @@
 ATTEND_CAP = 50.0
 LABEL_CAP = 30.0
 QUERY_SCALE = 1.0 / 12.0
+
+
+def gather_by_bits(shard, axis, dim):
+    ways, here = (lax.axis_size(axis), lax.axis_index(axis))
+    grown, reach = (shard, 1)
+    while reach < ways:
+        theirs = lax.ppermute(grown, axis, [(d, d ^ reach) for d in range(ways)])
+        mine_first = jnp.concatenate([grown, theirs], axis=dim)
+        theirs_first = jnp.concatenate([theirs, grown], axis=dim)
+        grown = jnp.where(here & reach == 0, mine_first, theirs_first)
+        reach = 2 * reach
+    return grown
 
 
 def rope_tables(positions, head_width):
@@ -68,7 +80,7 @@
     guard_rows = lax.all_to_all(whole_rows, "seq", split_axis=0, concat_axis=0, tiled=True)
     w_query, w_key, w_value, w_out = (
         lax.all_gather(query_weight, "seq", axis=0, tiled=True),
-        lax.all_gather(key_weight, "seq", axis=0, tiled=True),
+        gather_by_bits(key_weight, "seq", 0),
         lax.all_gather(value_weight, "seq", axis=0, tiled=True),
         lax.all_gather(out_weight, "seq", axis=1, tiled=True),
     )

time: 378 us -> 360 us (0.952)
  waiting for transfers between devices: 281 us -> 260 us
    ppermute x0 -> x3, waiting for transfers between devices: none -> 115 us  [gather_by_bits(): theirs = lax.ppermute(grown, axis, [(d, d ^ reach) for d in range(ways)])]
    all_gather x1, waiting for transfers between devices: 50 us -> 0.02 us  [shards(): lax.all_gather(value_weight, 'seq', axis=0, tiled=True)]
    all_gather x1, waiting for transfers between devices: 75.5 us -> 39.1 us  [shards(): lax.all_gather(query_weight, 'seq', axis=0, tiled=True)]
    all_gather x1 -> x0, waiting for transfers between devices: 25.5 us -> none  [shards(): lax.all_gather(key_weight, 'seq', axis=0, tiled=True)]
    all_to_all x1, waiting for transfers between devices: 24.1 us -> 0.01 us  [shards(): lax.all_to_all(whole_rows, 'seq', split_axis=0, concat_axis=0, tiled=True)]
    ppermute x0 -> x3, starting transfers between devices: none -> 5.11 us  [gather_by_bits(): theirs = lax.ppermute(grown, axis, [(d, d ^ reach) for d in range(ways)])]
  transfers between devices with their start and end apart: 7 -> 9, of which waited for: 7 -> 6; matrix products, arithmetic and copies ran while one was open for 7% -> 8% of each run, Pallas kernels for 0% -> 0%
where the time goes in v1:
time: 360 us
  waiting for transfers between devices  260 us (72%)
  matrix products  28.9 us (8%)
  blocking collectives  18.7 us (5%)
  local copies, waits for them, and re-layouts  16.4 us (5%)
  between operations  13.7 us (4%)
  other arithmetic  11.8 us (3%)
  starting transfers between devices  10.5 us (3%)
    ppermute x3, waiting for transfers between devices, gather_by_bits(): theirs = lax.ppermute(grown, axis, [(d, d ^ reach) for d in range(ways)])  115 us
    all_gather x1, waiting for transfers between devices, shards(): lax.all_gather(out_weight, 'seq', axis=1, tiled=True)  67.5 us
    all_gather x1, waiting for transfers between devices, shards(): lax.all_gather(query_weight, 'seq', axis=0, tiled=True)  39.1 us
    psum x1, waiting for transfers between devices, shards(): lax.psum(grad_part.astype(jnp.bfloat16), 'wg').astype(jnp.float32)  20.1 us
    all_to_all x1, blocking collectives, shards(): lax.all_to_all(grad_rows.astype(jnp.bfloat16), 'seq', split_axis=0, conca...  16.4 us
    psum x1, waiting for transfers between devices, shards(): lax.psum(out_part.astype(jnp.bfloat16), 'wg').astype(jnp.float32)  15.7 us
    dot_general x5, matrix products, times_transposed(): lax.dot_general(left_side, right_side, (((1,), (1,)), ((), ())), preferre...  8.46 us
  transfers between devices with their start and end apart: 9, of which 6 were waited for; matrix products, arithmetic and copies ran while one was open for 8% of the time, Pallas kernels for 0%

profile of v1, /device:TPU:0, one launch (start us, length us, event | category | flops | bytes accessed | tf_op | source)
XLA Modules:
  0.0 359.5 jit_solution(18335804989358486875)
XLA Ops:
  6.5 0.7 all-gather.6.cloned.1.call-update
  7.3 0.7 all-gather.4.cloned.1.call-update
  8.1 0.7 all-gather.8.cloned.1.call-update
  8.8 3.0 collective-permute-start
  11.8 2.3 all_gather.12
  14.1 5.0 %all-to-all-start = ((bf16[8,16,2304]{2,1,0:T(8,128)(2,1)}), bf16[8,16,2304]{2,1,0:T(8,128)(2,1)S(1)}, u32[]{:S(2)}, u32[]{:S(2)}) async-start(bf16[8,16,2304]{2,1,0:T(8,128)(2,1)} %bitcast), calls=%async_computation | async-start | bytes 1179648 | tf_op jit(solution)/shard_map/all_to_all | solution.py:80
  19.4 2.0 collective-permute-start.1
  21.5 0.6 dynamic_slice.10
  22.1 0.6 iota_compare_fusion.1
  23.0 39.3 %collective-permute-done.1 = bf16[576,512]{1,0:T(8,128)(2,1)S(1)} collective-permute-done((bf16[576,512]{1,0:T(8,128)(2,1)S(1)}, bf16[576,512]{1,0:T(8,128)(2,1)S(1)}, u32[]{:S(2)}, u32[]{:S(2)}) %collective-permute-start.1) | collective-permute-done | bytes 589856 | tf_op jit(solution)/shard_map/ppermute | solution.py:18
  62.4 0.5 maximum_select_fusion.1
  63.3 1.0 multiply_convert_fusion.2
  64.3 1.1 bitcast_convert_fusion
  65.5 75.6 %collective-permute-done.2 = bf16[1152,512]{1,0:T(8,128)(2,1)S(1)} collective-permute-done((bf16[1152,512]{1,0:T(8,128)(2,1)S(1)}, bf16[1152,512]{1,0:T(8,128)(2,1)S(1)}, u32[]{:S(2)}, u32[]{:S(2)}) %collective-permute-start.2) | collective-permute-done | bytes 1179680 | tf_op jit(solution)/shard_map/ppermute | solution.py:18
  141.1 1.0 copy-done.7
  142.1 1.8 fusion.35
  143.9 2.8 copy.41
  146.7 1.9 convolution_bitcast_fusion.3
  148.7 2.6 convolution_convert_fusion.3
  151.4 39.1 %all-gather.4.cloned.1.call-done = bf16[2304,1024]{1,0:T(8,128)(2,1)} async-done(((bf16[288,1024]{1,0:T(8,128)(2,1)}), bf16[2304,1024]{1,0:T(8,128)(2,1)}) %all-gather.4.cloned.1.call-update) | async-done | bytes 4718608 | tf_op jit(solution)/shard_map/all_gather | solution.py:82
  190.5 6.8 %copy.12 = bf16[1024,2304]{1,0:T(8,128)(2,1)} copy(bf16[1024,2304]{0,1:T(8,128)(2,1)} %bitcast.103) | data formatting | bytes 9437184 | tf_op jit(solution)/shard_map/dot_general | solution.py:100
  197.3 4.0 %convolution_bitcast_fusion = f32[8,128,128]{1,2,0:T(8,128)S(1)} fusion(bf16[128,2304,1]{1,0,2:T(8,128)(2,1)S(1)} %bitcast.109, bf16[8,128,2304]{2,1,0:T(8,128)(2,1)} %bitcast.106), kind=kOutput, calls=%fused_computation.17 | convolution fusion | flops 603979776 | bytes 5832704 | tf_op jit(solution)/shard_map/dot_general | solution.py:100
  202.1 0.4 fusion.34
  202.8 0.5 copy-done.20
  203.3 67.5 %all-gather.8.cloned.1.call-done = bf16[1024,2304]{0,1:T(8,128)(2,1)} async-done(((bf16[1024,288]{0,1:T(8,128)(2,1)}), bf16[1024,2304]{0,1:T(8,128)(2,1)}) %all-gather.8.cloned.1.call-update) | async-done | bytes 4718608 | tf_op jit(solution)/shard_map/all_gather | solution.py:85
  270.8 5.0 %convolution_convert_fusion = bf16[128,2304]{1,0:T(8,128)(2,1)} fusion(bf16[128,1024]{0,1:T(8,128)(2,1)S(1)} %bitcast.118, bf16[1024,2304]{0,1:T(8,128)(2,1)} %all-gather.8.cloned.1.call-done), kind=kOutput, calls=%fused_computation.5 | convolution fusion | flops 604274688 | bytes 5570560 | tf_op jit(solution)/shard_map/dot_general | solution.py:134
  276.0 0.6 dynamic_slice.11
  276.6 0.6 compare_convert_fusion
  277.2 15.7 %all-reduce.3.cloned.1.call-done = bf16[128,2304]{1,0:T(8,128)(2,1)} async-done(((bf16[128,2304]{1,0:T(8,128)(2,1)}), bf16[128,2304]{1,0:T(8,128)(2,1)}) %all-reduce.3.cloned.1.call-update) | async-done | bytes 589840 | tf_op jit(solution)/shard_map/psum | solution.py:135
  292.9 1.3 fusion.7
  294.2 1.6 multiply_reduce_fusion.2
  295.8 0.4 fusion.44
  296.3 0.5 multiply_reduce_fusion.1
  296.8 0.6 copy-done.1
  297.3 0.5 fusion.13
  297.9 1.1 convolution_convert_fusion.2
  299.1 1.4 fusion.14
  300.8 1.7 convolution_bitcast_fusion.2
  302.5 2.5 convolution_multiply_fusion.1
  305.1 1.2 copy.24
  306.5 4.2 %fusion.68 = f32[128,2304]{1,0:T(8,128)S(1)} fusion(bf16[128,1024]{0,1:T(8,128)(2,1)S(1)} %bitcast.117, bf16[2304,1024]{1,0:T(8,128)(2,1)} %all-gather.4.cloned.1.call-done), kind=kOutput, calls=%fused_computation.126 | convolution fusion | flops 603979776 | bytes 6160384 | tf_op jit(solution)/shard_map/dot_general | solution.py:59
  310.7 0.9 convolution_add_fusion.1
  311.7 0.7 copy-done.2
  312.4 1.8 fusion.1
  314.2 20.1 %all-reduce.5.cloned.1.call-done = bf16[128,2304]{1,0:T(8,128)(2,1)} async-done(((bf16[128,2304]{1,0:T(8,128)(2,1)}), bf16[128,2304]{1,0:T(8,128)(2,1)}) %all-reduce.5.cloned.1.call-update) | async-done | bytes 589840 | tf_op jit(solution)/shard_map/psum | solution.py:190
  334.3 1.3 multiply_reduce_fusion
  335.9 16.4 %all_to_all.21 = bf16[8,16,1152]{2,1,0:T(8,128)(2,1)S(1)} all-to-all(bf16[8,16,1152]{2,1,0:T(8,128)(2,1)S(1)} %bitcast.111), channel_id=1, replica_groups=mesh['groups'=2,'seq'=8,'wg'=2] {'seq'}, dimensions={0} | all-to-all | bytes 589824 | tf_op jit(solution)/shard_map/all_to_all | solution.py:195
  352.3 0.7 copy.55
  (82 shorter events, 3.2 us)
Async XLA Ops:
  6.5 289.3 %copy-start = (bf16[64,2304]{1,0:T(8,128)(2,1)S(1)}, bf16[64,2304]{1,0:T(8,128)(2,1)}, u32[]{:S(2)}) copy-start(bf16[64,2304]{1,0:T(8,128)(2,1)} %param.19) | copy-start | bytes 884740
  6.5 2.2 copy-start.10
  6.5 5.2 %copy-start.9 = (bf16[128,1152]{1,0:T(8,128)(2,1)S(1)}, bf16[128,1152]{1,0:T(8,128)(2,1)}, u32[]{:S(2)}) copy-start(bf16[128,1152]{1,0:T(8,128)(2,1)} %param.11) | copy-start | bytes 884740
  6.5 142.1 %all-gather.6.cloned.1.call-start = ((), (), s32[]{:S(2)}) async-start(), calls=%async_computation.3 | async-start | bytes 2654208 | tf_op jit(solution)/shard_map/all_gather | solution.py:84
  7.3 183.2 %all-gather.4.cloned.1.call-start = ((), (), s32[]{:S(2)}) async-start(), calls=%async_computation.2 | async-start | bytes 5308416 | tf_op jit(solution)/shard_map/all_gather | solution.py:82
  8.0 262.7 %all-gather.8.cloned.1.call-start = ((), (), s32[]{:S(2)}) async-start(), calls=%async_computation.4 | async-start | bytes 5308416 | tf_op jit(solution)/shard_map/all_gather | solution.py:85
  8.8 10.4 %collective-permute-start = (bf16[288,512]{1,0:T(8,128)(2,1)S(1)}, bf16[288,512]{1,0:T(8,128)(2,1)S(1)}, u32[]{:S(2)}, u32[]{:S(2)}) collective-permute-start(bf16[288,512]{1,0:T(8,128)(2,1)S(1)} %copy-done.10), channel_id=1, source_target_pairs={{0,2},{2,0},{4,6},{6,4},{8,10},{10,8},{12,14},{14,12},{1,3},{3,1},... | collective-permute-start | bytes 884744 | tf_op jit(solution)/shard_map/ppermute | solution.py:18
  14.1 7.4 %copy-start.18 = (s32[8]{0:T(128)S(1)}, s32[8]{0:T(128)}, u32[]{:S(2)}) copy-start(s32[8]{0:T(128)} %param.20) | copy-start | bytes 100
  14.1 48.9 %all-to-all-start = ((bf16[8,16,2304]{2,1,0:T(8,128)(2,1)}), bf16[8,16,2304]{2,1,0:T(8,128)(2,1)S(1)}, u32[]{:S(2)}, u32[]{:S(2)}) async-start(bf16[8,16,2304]{2,1,0:T(8,128)(2,1)} %bitcast), calls=%async_computation | async-start | bytes 1179648 | tf_op jit(solution)/shard_map/all_to_all | solution.py:80
  19.1 273.8 %all-reduce.3.cloned.1.call-start = ((), (), s32[]{:S(2)}) async-start(), calls=%async_computation.5 | async-start | bytes 1179648 | tf_op jit(solution)/shard_map/psum | solution.py:135
  19.4 42.9 %collective-permute-start.1 = (bf16[576,512]{1,0:T(8,128)(2,1)S(1)}, bf16[576,512]{1,0:T(8,128)(2,1)S(1)}, u32[]{:S(2)}, u32[]{:S(2)}) collective-permute-start(bf16[576,512]{1,0:T(8,128)(2,1)S(1)} %maximum_select_fusion.2), channel_id=1, source_target_pairs={{0,4},{2,6},{4,0},{6,2},{8,12},{10,14},{12,8},{14,10},{1,5},{3,7},... | collective-permute-start | bytes 1769480 | tf_op jit(solution)/shard_map/ppermute | solution.py:18
  23.0 40.2 %copy-start.13 = (f32[2304]{0:T(1024)S(1)}, f32[2304]{0:T(1024)}, u32[]{:S(2)}) copy-start(f32[2304]{0:T(1024)} %param.12) | copy-start | bytes 27652
  62.9 78.2 %copy-start.5 = (bf16[1152,512]{1,0:T(8,128)(2,1)}, bf16[1152,512]{1,0:T(8,128)(2,1)S(1)}, u32[]{:S(2)}) copy-start(bf16[1152,512]{1,0:T(8,128)(2,1)S(1)} %maximum_select_fusion.1) | copy-start | bytes 3538948
  62.9 78.2 %collective-permute-start.2 = (bf16[1152,512]{1,0:T(8,128)(2,1)S(1)}, bf16[1152,512]{1,0:T(8,128)(2,1)S(1)}, u32[]{:S(2)}, u32[]{:S(2)}) collective-permute-start(bf16[1152,512]{1,0:T(8,128)(2,1)S(1)} %maximum_select_fusion.1), channel_id=1, source_target_pairs={{0,8},{2,10},{4,12},{6,14},{8,0},{10,2},{12,4},{14,6},{1,9},{3,11}... | collective-permute-start | bytes 3538952 | tf_op jit(solution)/shard_map/ppermute | solution.py:18
  141.1 1.0 copy-start.7
  148.6 53.5 %copy-start.15 = (bf16[4,128,64]{1,2,0:T(8,128)(2,1)}, bf16[4,128,64]{1,2,0:T(8,128)(2,1)S(1)}, u32[]{:S(2)}) copy-start(bf16[4,128,64]{1,2,0:T(8,128)(2,1)S(1)} %get-tuple-element.18) | copy-start | bytes 196612
  190.5 6.8 %copy-start.4 = (bf16[8,16,2304]{2,1,0:T(8,128)(2,1)S(1)}, bf16[8,16,2304]{2,1,0:T(8,128)(2,1)}, u32[]{:S(2)}) copy-start(bf16[8,16,2304]{2,1,0:T(8,128)(2,1)} %multiply_convert_fusion.2) | copy-start | bytes 1769476
  202.1 0.7 copy-start.11
  202.5 0.8 copy-start.20
  270.8 5.2 %copy-start.19 = (s32[8]{0:T(128)S(1)}, s32[8]{0:T(128)}, u32[]{:S(2)}) copy-start(s32[8]{0:T(128)} %param.21) | copy-start | bytes 100
  270.8 27.1 %slice-start = ((s8[4718592]{0:T(1024)(128)(4,1)}), s8[524288]{0:T(1024)(128)(4,1)S(1)}, s32[]{:S(2)}) async-start(s8[4718592]{0:T(1024)(128)(4,1)} %bitcast.104), calls=%async_computation.7 | async-start | bytes 1048576
  275.7 18.5 %copy-start.14 = (f32[2304]{0:T(1024)S(1)}, f32[2304]{0:T(1024)}, u32[]{:S(2)}) copy-start(f32[2304]{0:T(1024)} %param.17) | copy-start | bytes 27652
  275.7 20.1 %copy-start.17 = (f32[2304]{0:T(1024)S(1)}, f32[2304]{0:T(1024)}, u32[]{:S(2)}) copy-start(f32[2304]{0:T(1024)} %param.18) | copy-start | bytes 27652
  275.7 58.6 %all-reduce.5.cloned.1.call-start = ((), (), s32[]{:S(2)}) async-start(), calls=%async_computation.6 | async-start | bytes 1179648 | tf_op jit(solution)/shard_map/psum | solution.py:190
  294.2 3.7 %slice-start.1 = ((s8[4718592]{0:T(1024)(128)(4,1)}), s8[4194304]{0:T(1024)(128)(4,1)S(1)}, s32[]{:S(2)}) async-start(s8[4718592]{0:T(1024)(128)(4,1)} %bitcast.104), calls=%async_computation.8 | async-start | bytes 8388608
  296.3 1.1 copy-start.1
  299.1 1.6 copy-start.12
  300.7 1.7 copy-start.16
  306.4 4.2 %copy-start.6 = (bf16[1152,512]{1,0:T(8,128)(2,1)S(1)}, bf16[1152,512]{1,0:T(8,128)(2,1)}, u32[]{:S(2)}) copy-start(bf16[1152,512]{1,0:T(8,128)(2,1)} %copy-done.5) | copy-start | bytes 3538948
  306.4 4.2 %copy-start.8 = (bf16[1152,512]{1,0:T(8,128)(2,1)S(1)}, bf16[1152,512]{1,0:T(8,128)(2,1)}, u32[]{:S(2)}) copy-start(bf16[1152,512]{1,0:T(8,128)(2,1)} %copy-done.7) | copy-start | bytes 3538948
  310.7 1.7 copy-start.2
  314.2 21.5 %copy-start.3 = (f32[128,2304]{1,0:T(8,128)S(1)}, f32[128,2304]{1,0:T(8,128)}, u32[]{:S(2)}) copy-start(f32[128,2304]{1,0:T(8,128)} %bitcast_convert_fusion) | copy-start | bytes 3538948
Sparse Core Ops, SparseCore 0:
  9.5 92.7 all-gather.5
  104.5 85.9 all-gather.3
  192.7 78.0 all-gather.7
  275.9 16.9 all-reduce.2
  314.3 20.0 all-reduce.4
